TPU v7x, 32 devices: a whole 2x2x4 slice. The times are simulated.
32 devices in a mesh: seq: 8 (over y, x, core), fsdp: 4 (over z).
Axes of the slice: x: 2, y: 2, z: 4, core: 2. Of those that a mesh axis runs over, the one named last changes fastest.
Arguments:
- query_states: bfloat16 [2048, 4096], P('seq', 'fsdp'), may hold values from -24 to 24
- key_states: bfloat16 [2048, 4096], P('seq', 'fsdp'), may hold values from -6 to 6
- value_states: bfloat16 [2048, 4096], P('seq', 'fsdp'), may hold values from -6 to 6
- positions: int32 [2048], P('seq'), may hold values from 0 to 2047, as said below
- out_weight: bfloat16 [4096, 5120], P('fsdp', 'seq'), may hold values from -1 to 1
- cotangent: bfloat16 [2048, 5120], P('seq', 'fsdp'), may hold values from -0.59765625 to 0.59765625
Outputs:
- attn_output: float32 [2048, 5120], P('seq', 'fsdp')
- grad_queries: float32 [2048, 4096], P('seq', 'fsdp')
- grad_keys: float32 [2048, 4096], P('seq', 'fsdp')
- grad_values: float32 [2048, 4096], P('seq', 'fsdp')
- grad_weight: float32 [4096, 5120], P('fsdp', 'seq')
Inputs may be any that keep to these rules, and one draw needn't show every extreme that they name: A permutation of 0 to 2047; each aligned block of 256 rows holds, in increasing order, the positions of one residue class modulo 2048 // 256.
All inputs are finite; a program needn't handle non-finite values.
Results may differ from a plain program's by a relative error of at most 0.02.
Values may be sent and summed in bfloat16 or wider, within the bound.
No kernel may reach another device: no remote copies, remote signals or barrier semaphores. Data moves between devices by JAX's collectives and lax.ppermute only.
A program may use at most 128 MiB of HBM per device.

v0:
```python
import jax
import jax.numpy as jnp
from jax import lax
from jax.sharding import PartitionSpec as P

HEAD_DIM = 128
blocked = -1e30


def shifted(block, axis, distance):
    devices = range(lax.axis_size(axis))
    route = [((i - distance) % len(devices), i) for i in devices]
    return lax.ppermute(block, axis, route)


def split_heads(matrix):
    return matrix.reshape(matrix.shape[0], -1, HEAD_DIM)


def masked_scores(query_rows, key_rows, query_pos, key_pos):
    raw = jnp.einsum(
        "qhd,khd->hqk", query_rows, key_rows, preferred_element_type=jnp.float32
    ) * HEAD_DIM ** (-0.5)
    visible = key_pos[None, None, :] <= query_pos[None, :, None]
    return jnp.where(visible, raw, blocked)


def tile_grads(
    query_rows, grad_rows, log_total, row_delta, query_pos, key_rows, value_rows, key_pos
):
    scores = masked_scores(query_rows, key_rows, query_pos, key_pos)
    probs = jnp.exp(scores - log_total[:, :, None])
    grad_probs = jnp.einsum(
        "qhd,khd->hqk", grad_rows, value_rows, preferred_element_type=jnp.float32
    )
    grad_scores = (probs * (grad_probs - row_delta[:, :, None])).astype(jnp.bfloat16)
    grad_query = jnp.einsum(
        "hqk,khd->qhd", grad_scores, key_rows, preferred_element_type=jnp.float32
    )
    grad_key = jnp.einsum(
        "hqk,qhd->khd", grad_scores, query_rows, preferred_element_type=jnp.float32
    )
    grad_value = jnp.einsum(
        "hqk,qhd->khd", probs.astype(jnp.bfloat16), grad_rows, preferred_element_type=jnp.float32
    )
    return (grad_query, grad_key, grad_value)


def shards(query_states, key_states, value_states, positions, out_weight, cotangent):
    local_tokens = query_states.shape[0]
    query_heads = split_heads(query_states)
    key_heads = split_heads(key_states)
    value_heads = split_heads(value_states)
    local_heads = query_heads.shape[1]
    row_max = jnp.full((local_heads, local_tokens), blocked, jnp.float32)
    piece_keys = lax.all_gather(key_states, "seq", axis=0, tiled=True)
    piece_pos = lax.all_gather(positions, "seq", axis=0, tiled=True)
    scores = masked_scores(query_heads, split_heads(piece_keys), positions, piece_pos)
    new_max = jnp.maximum(row_max, jnp.max(scores, axis=2))
    new_total = jnp.sum(jnp.exp(scores - new_max[:, :, None]), axis=2)
    log_total = new_max + jnp.log(new_total)
    zero_heads = jnp.zeros((local_tokens, local_heads, HEAD_DIM), jnp.float32)
    piece_keys = lax.all_gather(key_states, "seq", axis=0, tiled=True)
    piece_values = lax.all_gather(value_states, "seq", axis=0, tiled=True)
    piece_pos = lax.all_gather(positions, "seq", axis=0, tiled=True)
    scores = masked_scores(query_heads, split_heads(piece_keys), positions, piece_pos)
    weights = jnp.exp(scores - log_total[:, :, None]).astype(jnp.bfloat16)
    attended = jnp.einsum(
        "hqk,khd->qhd", weights, split_heads(piece_values), preferred_element_type=jnp.float32
    )
    attended_heads = attended.astype(jnp.bfloat16)
    attended_flat = attended_heads.reshape(local_tokens, local_heads * HEAD_DIM)
    weight_full = lax.all_gather(out_weight, "seq", axis=1, tiled=True)
    partial_sum = jnp.dot(attended_flat, weight_full, preferred_element_type=jnp.float32).astype(
        jnp.bfloat16
    )
    attn_output = lax.psum_scatter(partial_sum, "fsdp", scatter_dimension=1, tiled=True).astype(
        jnp.float32
    )
    cotangent_full = lax.all_gather(cotangent, "fsdp", axis=1, tiled=True)
    grad_attended = jnp.einsum(
        "td,hd->th", cotangent_full, weight_full, preferred_element_type=jnp.float32
    ).astype(jnp.bfloat16)
    weight_term = jnp.einsum(
        "th,td->hd", attended_flat, cotangent_full, preferred_element_type=jnp.float32
    )
    grad_weight = lax.psum_scatter(weight_term, "seq", scatter_dimension=1, tiled=True)
    grad_heads = split_heads(grad_attended)
    row_delta = jnp.sum(
        grad_heads.astype(jnp.float32) * attended_heads.astype(jnp.float32), axis=2
    ).T
    cycle_length = lax.axis_size("seq")

    def key_step(cycle_step, state_tuple):
        key_block, value_block, key_pos, key_grad, value_grad, query_grad = state_tuple
        grad_query, grad_key, grad_value = tile_grads(
            query_heads,
            grad_heads,
            log_total,
            row_delta,
            positions,
            key_block,
            value_block,
            key_pos,
        )
        key_block, value_block, key_pos = shifted((key_block, value_block, key_pos), "seq", 1)
        key_grad, value_grad = shifted((key_grad + grad_key, value_grad + grad_value), "seq", 1)
        return (key_block, value_block, key_pos, key_grad, value_grad, query_grad + grad_query)

    final_state = lax.fori_loop(
        0,
        cycle_length,
        key_step,
        (key_heads, value_heads, positions, zero_heads, zero_heads, zero_heads),
    )
    query_sum, key_sum, value_sum = (final_state[5], final_state[3], final_state[4])
    score_scale = HEAD_DIM ** (-0.5)
    grad_queries = (query_sum * score_scale).reshape(local_tokens, local_heads * HEAD_DIM)
    grad_keys = (key_sum * score_scale).reshape(local_tokens, local_heads * HEAD_DIM)
    grad_values = value_sum.reshape(local_tokens, local_heads * HEAD_DIM)
    return (attn_output, grad_queries, grad_keys, grad_values, grad_weight)


def solution(mesh):
    in_specs = (
        P("seq", "fsdp"),
        P("seq", "fsdp"),
        P("seq", "fsdp"),
        P("seq"),
        P("fsdp", "seq"),
        P("seq", "fsdp"),
    )
    out_specs = (
        P("seq", "fsdp"),
        P("seq", "fsdp"),
        P("seq", "fsdp"),
        P("seq", "fsdp"),
        P("fsdp", "seq"),
    )
    return jax.shard_map(shards, mesh=mesh, in_specs=in_specs, out_specs=out_specs, check_vma=False)
```

profile of v0, /device:TPU:0, one launch (start us, length us, event | category | flops | bytes accessed | tf_op | source)
XLA Modules:
  0.0 683.8 jit_solution(8055189785752940412)
XLA Ops:
  11.6 10.4 %all-gather = s32[8,1,256]{2,1,0:T(1,128)S(1)} all-gather(s32[1,1,256]{2,1,0:T(1,128)S(1)} %bitcast.97), channel_id=1, replica_groups=mesh['seq'=8,'fsdp'=4] {'seq'}, dimensions={0}, use_global_device_ids=true | all-gather | bytes 9216 | tf_op jit(solution)/shard_map/all_gather | solution.py:65
  22.4 26.8 %all-gather.8.cloned.1.call-done = bf16[2048,1024]{1,0:T(8,128)(2,1)} async-done(((bf16[256,1024]{1,0:T(8,128)(2,1)}), bf16[2048,1024]{1,0:T(8,128)(2,1)}) %all-gather.8.cloned.1.call-update) | async-done | bytes 4194320 | tf_op jit(solution)/shard_map/all_gather | solution.py:64
  49.2 6.5 copy.42
  55.7 33.3 %all-gather.6.cloned.1.call-done = bf16[2048,1024]{0,1:T(8,128)(2,1)} async-done(((bf16[256,1024]{0,1:T(8,128)(2,1)}), bf16[2048,1024]{0,1:T(8,128)(2,1)}) %all-gather.6.cloned.1.call-update) | async-done | bytes 4194320 | tf_op jit(solution)/shard_map/all_gather | solution.py:63
  89.0 5.3 fusion.4
  94.3 4.5 exponential_reduce_fusion
  100.5 44.9 %all-gather.12.cloned.1.call-done = bf16[256,5120]{1,0:T(8,128)(2,1)} async-done(((bf16[256,1280]{1,0:T(8,128)(2,1)}), bf16[256,5120]{1,0:T(8,128)(2,1)}) %all-gather.12.cloned.1.call-update) | async-done | bytes 2621456 | tf_op jit(solution)/shard_map/all_gather | solution.py:80
  145.4 63.5 %all-gather.10.cloned.1.call-done = bf16[1024,5120]{1,0:T(8,128)(2,1)} async-done(((bf16[1024,640]{1,0:T(8,128)(2,1)}), bf16[1024,5120]{1,0:T(8,128)(2,1)}) %all-gather.10.cloned.1.call-update) | async-done | bytes 10485776 | tf_op jit(solution)/shard_map/all_gather | solution.py:73
  208.9 8.5 %convolution_convert_fusion.1 = bf16[256,1024]{1,0:T(8,128)(2,1)} fusion(bf16[256,5120]{1,0:T(8,128)(2,1)} %all-gather.12.cloned.1.call-done, bf16[1024,5120]{1,0:T(8,128)(2,1)} %all-gather.10.cloned.1.call-done), kind=kOutput, calls=%fused_computation.18 | convolution fusion | flops 2684616704 | bytes 13631488 | tf_op jit(solution)/shard_map/td,hd->th/dot_general | solution.py:81
  219.6 9.9 %multiply_reduce_fusion = (f32[256,8]{0,1:T(8,128)S(1)}, bf16[8,256,128]{1,2,0:T(8,128)(2,1)S(1)}) fusion(bf16[256,1024]{0,1:T(8,128)(2,1)} %copy.45, bf16[2048,8,128]{0,2,1:T(8,128)(2,1)} %bitcast.89, f32[8,256,2048]{2,1,0:T(8,128)} %copy-done, f32[8,256]{1,0:T(8,128)S(1)} %log_add_fusion, pred[256,2048]{1,0:T(8,128)(4,1)S(1)} %broadcast_compare_fusion.1), kind=kOutput, calls=%fused_computation.24 | convolution fusion | flops 1091827712 | bytes 22560768 | tf_op jit(solution)/shard_map/hqk,khd->qhd/dot_general | solution.py:68
  230.3 4.3 convolution_convert_fusion
  236.3 9.8 %fusion.10 = f32[1024,5120]{1,0:T(8,128)} fusion(bf16[256,1024]{0,1:T(8,128)(2,1)} %bitcast.91, bf16[256,5120]{1,0:T(8,128)(2,1)S(1)} %copy-done.3), kind=kOutput, calls=%fused_computation.30 | convolution fusion | flops 2684354560 | bytes 24117248 | tf_op jit(solution)/shard_map/th,td->hd/dot_general | solution.py:84
  251.9 416.6 %while.21 = (s32[]{:T(128)}, bf16[256,8,128]{2,0,1:T(8,128)(2,1)}, bf16[256,8,128]{2,0,1:T(8,128)(2,1)}, s32[256]{0:T(256)S(1)}, f32[256,8,128]{2,0,1:T(8,128)},...) while((s32[]{:T(128)}, bf16[256,8,128]{2,0,1:T(8,128)(2,1)}, ...), condition=%wide.region_5.6_spmd.clone, body=%wide.region_4.5_spmd.clone.sunk | while | flops 675872768 | bytes 34234708 | solution.py:110
  258.4 2.7 fusion.54
  265.4 30.6 %collective-permute-done.2 = s32[256]{0:T(256)S(1)} collective-permute-done((s32[256]{0:T(256)S(1)}, s32[256]{0:T(256)S(1)}, u32[]{:S(2)}, u32[]{:S(2)}) %collective-permute-start.2) | collective-permute-done | bytes 1056 | tf_op jit(solution)/shard_map/while/body/eval_jaxpr/ppermute | solution.py:13
  299.6 2.9 fusion.53
  302.4 2.9 fusion.54
  308.6 2.8 fusion.55
  311.4 43.0 %collective-permute-done.2 = s32[256]{0:T(256)S(1)} collective-permute-done((s32[256]{0:T(256)S(1)}, s32[256]{0:T(256)S(1)}, u32[]{:S(2)}, u32[]{:S(2)}) %collective-permute-start.2) | collective-permute-done | bytes 1056 | tf_op jit(solution)/shard_map/while/body/eval_jaxpr/ppermute | solution.py:13
  360.7 2.7 fusion.54
  365.1 3.4 collective-permute-start.1
  371.1 75.8 %collective-permute-done.2 = s32[256]{0:T(256)S(1)} collective-permute-done((s32[256]{0:T(256)S(1)}, s32[256]{0:T(256)S(1)}, u32[]{:S(2)}, u32[]{:S(2)}) %collective-permute-start.2) | collective-permute-done | bytes 1056 | tf_op jit(solution)/shard_map/while/body/eval_jaxpr/ppermute | solution.py:13
  457.5 3.4 collective-permute-start.1
  463.6 28.4 %collective-permute-done.2 = s32[256]{0:T(256)S(1)} collective-permute-done((s32[256]{0:T(256)S(1)}, s32[256]{0:T(256)S(1)}, u32[]{:S(2)}, u32[]{:S(2)}) %collective-permute-start.2) | collective-permute-done | bytes 1056 | tf_op jit(solution)/shard_map/while/body/eval_jaxpr/ppermute | solution.py:13
  501.6 3.5 collective-permute-start.1
  507.7 28.4 %collective-permute-done.2 = s32[256]{0:T(256)S(1)} collective-permute-done((s32[256]{0:T(256)S(1)}, s32[256]{0:T(256)S(1)}, u32[]{:S(2)}, u32[]{:S(2)}) %collective-permute-start.2) | collective-permute-done | bytes 1056 | tf_op jit(solution)/shard_map/while/body/eval_jaxpr/ppermute | solution.py:13
  545.7 3.4 collective-permute-start.1
  551.8 28.4 %collective-permute-done.2 = s32[256]{0:T(256)S(1)} collective-permute-done((s32[256]{0:T(256)S(1)}, s32[256]{0:T(256)S(1)}, u32[]{:S(2)}, u32[]{:S(2)}) %collective-permute-start.2) | collective-permute-done | bytes 1056 | tf_op jit(solution)/shard_map/while/body/eval_jaxpr/ppermute | solution.py:13
  589.8 3.4 collective-permute-start.1
  595.9 28.4 %collective-permute-done.2 = s32[256]{0:T(256)S(1)} collective-permute-done((s32[256]{0:T(256)S(1)}, s32[256]{0:T(256)S(1)}, u32[]{:S(2)}, u32[]{:S(2)}) %collective-permute-start.2) | collective-permute-done | bytes 1056 | tf_op jit(solution)/shard_map/while/body/eval_jaxpr/ppermute | solution.py:13
  633.9 3.4 collective-permute-start.1
  640.0 28.4 %collective-permute-done.2 = s32[256]{0:T(256)S(1)} collective-permute-done((s32[256]{0:T(256)S(1)}, s32[256]{0:T(256)S(1)}, u32[]{:S(2)}, u32[]{:S(2)}) %collective-permute-start.2) | collective-permute-done | bytes 1056 | tf_op jit(solution)/shard_map/while/body/eval_jaxpr/ppermute | solution.py:13
  (190 shorter events, 115.1 us)
Async XLA Ops:
  7.2 42.0 %all-gather.8.cloned.1.call-start = ((), (), s32[]{:S(2)}) async-start(), calls=%async_computation.3 | async-start | bytes 4718592 | tf_op jit(solution)/shard_map/all_gather | solution.py:64
  7.9 81.1 %all-gather.6.cloned.1.call-start = ((), (), s32[]{:S(2)}) async-start(), calls=%async_computation.2 | async-start | bytes 4718592 | tf_op jit(solution)/shard_map/all_gather | solution.py:63
  10.0 135.4 %all-gather.12.cloned.1.call-start = ((), (), s32[]{:S(2)}) async-start(), calls=%async_computation.6 | async-start | bytes 3276800 | tf_op jit(solution)/shard_map/all_gather | solution.py:80
  10.8 198.2 %all-gather.10.cloned.1.call-start = ((), (), s32[]{:S(2)}) async-start(), calls=%async_computation.4 | async-start | bytes 11796480 | tf_op jit(solution)/shard_map/all_gather | solution.py:73
  11.3 663.4 %reduce-scatter.3.cloned.1.call-start = ((), (), s32[]{:S(2)}) async-start(), calls=%async_computation.5 | async-start | bytes 3276800 | tf_op jit(solution)/shard_map/reduce_scatter | solution.py:77
  234.6 442.4 %reduce-scatter.5.cloned.1.call-start = ((), (), s32[]{:S(2)}) async-start(), calls=%async_computation.7 | async-start | bytes 23592960 | tf_op jit(solution)/shard_map/reduce_scatter | solution.py:87
  258.1 37.9 %collective-permute-start.3 = (f32[256,8,128]{2,0,1:T(8,128)}, f32[256,8,128]{2,0,1:T(8,128)}, u32[]{:S(2)}, u32[]{:S(2)}) collective-permute-start(f32[256,8,128]{2,0,1:T(8,128)} %fusion.53), channel_id=1, source_target_pairs={{28,0},{0,4},{4,8},{8,12},{12,16},{16,20},{20,24},{24,28},{29,1},{... | collective-permute-start | bytes 3145736 | tf_op jit(solution)/shard_map/while/body/eval_jaxpr/ppermute | solution.py:13
  302.4 52.0 %collective-permute-start.3 = (f32[256,8,128]{2,0,1:T(8,128)}, f32[256,8,128]{2,0,1:T(8,128)}, u32[]{:S(2)}, u32[]{:S(2)}) collective-permute-start(f32[256,8,128]{2,0,1:T(8,128)} %fusion.53), channel_id=1, source_target_pairs={{28,0},{0,4},{4,8},{8,12},{12,16},{16,20},{20,24},{24,28},{29,1},{... | collective-permute-start | bytes 3145736 | tf_op jit(solution)/shard_map/while/body/eval_jaxpr/ppermute | solution.py:13
  305.4 49.0 %collective-permute-start.4 = (f32[256,8,128]{2,0,1:T(8,128)}, f32[256,8,128]{2,0,1:T(8,128)}, u32[]{:S(2)}, u32[]{:S(2)}) collective-permute-start(f32[256,8,128]{2,0,1:T(8,128)} %fusion.54), channel_id=1, source_target_pairs={{28,0},{0,4},{4,8},{8,12},{12,16},{16,20},{20,24},{24,28},{29,1},{... | collective-permute-start | bytes 3145736 | tf_op jit(solution)/shard_map/while/body/eval_jaxpr/ppermute | solution.py:13
  306.3 48.0 %collective-permute-start = (bf16[256,8,128]{2,0,1:T(8,128)(2,1)S(1)}, bf16[256,8,128]{2,0,1:T(8,128)(2,1)}, u32[]{:S(2)}, u32[]{:S(2)}) collective-permute-start(bf16[256,8,128]{2,0,1:T(8,128)(2,1)S(1)} %copy.73), channel_id=1, source_target_pairs={{28,0},{0,4},{4,8},{8,12},{12,16},{16,20},{20,24},{24,28},{29,1},{... | collective-permute-start | bytes 1572872 | tf_op jit(solution)/shard_map/while/body/eval_jaxpr/ppermute | solution.py:13
  306.4 48.0 %collective-permute-start.1 = (bf16[256,8,128]{2,0,1:T(8,128)(2,1)S(1)}, bf16[256,8,128]{2,0,1:T(8,128)(2,1)}, u32[]{:S(2)}, u32[]{:S(2)}) collective-permute-start(bf16[256,8,128]{2,0,1:T(8,128)(2,1)S(1)} %copy.74), channel_id=1, source_target_pairs={{28,0},{0,4},{4,8},{8,12},{12,16},{16,20},{20,24},{24,28},{29,1},{... | collective-permute-start | bytes 1572872 | tf_op jit(solution)/shard_map/while/body/eval_jaxpr/ppermute | solution.py:13
  308.5 45.9 %collective-permute-start.2 = (s32[256]{0:T(256)S(1)}, s32[256]{0:T(256)S(1)}, u32[]{:S(2)}, u32[]{:S(2)}) collective-permute-start(s32[256]{0:T(256)S(1)} %copy.75), channel_id=1, source_target_pairs={{28,0},{0,4},{4,8},{8,12},{12,16},{16,20},{20,24},{24,28},{29,1},{... | collective-permute-start | bytes 3080 | tf_op jit(solution)/shard_map/while/body/eval_jaxpr/ppermute | solution.py:13
  360.7 86.3 %collective-permute-start.3 = (f32[256,8,128]{2,0,1:T(8,128)}, f32[256,8,128]{2,0,1:T(8,128)}, u32[]{:S(2)}, u32[]{:S(2)}) collective-permute-start(f32[256,8,128]{2,0,1:T(8,128)} %fusion.53), channel_id=1, source_target_pairs={{28,0},{0,4},{4,8},{8,12},{12,16},{16,20},{20,24},{24,28},{29,1},{... | collective-permute-start | bytes 3145736 | tf_op jit(solution)/shard_map/while/body/eval_jaxpr/ppermute | solution.py:13
  363.4 83.6 %collective-permute-start.4 = (f32[256,8,128]{2,0,1:T(8,128)}, f32[256,8,128]{2,0,1:T(8,128)}, u32[]{:S(2)}, u32[]{:S(2)}) collective-permute-start(f32[256,8,128]{2,0,1:T(8,128)} %fusion.54), channel_id=1, source_target_pairs={{28,0},{0,4},{4,8},{8,12},{12,16},{16,20},{20,24},{24,28},{29,1},{... | collective-permute-start | bytes 3145736 | tf_op jit(solution)/shard_map/while/body/eval_jaxpr/ppermute | solution.py:13
  364.7 82.3 %collective-permute-start = (bf16[256,8,128]{2,0,1:T(8,128)(2,1)S(1)}, bf16[256,8,128]{2,0,1:T(8,128)(2,1)}, u32[]{:S(2)}, u32[]{:S(2)}) collective-permute-start(bf16[256,8,128]{2,0,1:T(8,128)(2,1)S(1)} %copy.73), channel_id=1, source_target_pairs={{28,0},{0,4},{4,8},{8,12},{12,16},{16,20},{20,24},{24,28},{29,1},{... | collective-permute-start | bytes 1572872 | tf_op jit(solution)/shard_map/while/body/eval_jaxpr/ppermute | solution.py:13
  365.1 81.9 %collective-permute-start.1 = (bf16[256,8,128]{2,0,1:T(8,128)(2,1)S(1)}, bf16[256,8,128]{2,0,1:T(8,128)(2,1)}, u32[]{:S(2)}, u32[]{:S(2)}) collective-permute-start(bf16[256,8,128]{2,0,1:T(8,128)(2,1)S(1)} %copy.74), channel_id=1, source_target_pairs={{28,0},{0,4},{4,8},{8,12},{12,16},{16,20},{20,24},{24,28},{29,1},{... | collective-permute-start | bytes 1572872 | tf_op jit(solution)/shard_map/while/body/eval_jaxpr/ppermute | solution.py:13
  368.5 78.5 %collective-permute-start.2 = (s32[256]{0:T(256)S(1)}, s32[256]{0:T(256)S(1)}, u32[]{:S(2)}, u32[]{:S(2)}) collective-permute-start(s32[256]{0:T(256)S(1)} %copy.75), channel_id=1, source_target_pairs={{28,0},{0,4},{4,8},{8,12},{12,16},{16,20},{20,24},{24,28},{29,1},{... | collective-permute-start | bytes 3080 | tf_op jit(solution)/shard_map/while/body/eval_jaxpr/ppermute | solution.py:13
  453.2 38.9 %collective-permute-start.3 = (f32[256,8,128]{2,0,1:T(8,128)}, f32[256,8,128]{2,0,1:T(8,128)}, u32[]{:S(2)}, u32[]{:S(2)}) collective-permute-start(f32[256,8,128]{2,0,1:T(8,128)} %fusion.53), channel_id=1, source_target_pairs={{28,0},{0,4},{4,8},{8,12},{12,16},{16,20},{20,24},{24,28},{29,1},{... | collective-permute-start | bytes 3145736 | tf_op jit(solution)/shard_map/while/body/eval_jaxpr/ppermute | solution.py:13
  455.9 36.2 %collective-permute-start.4 = (f32[256,8,128]{2,0,1:T(8,128)}, f32[256,8,128]{2,0,1:T(8,128)}, u32[]{:S(2)}, u32[]{:S(2)}) collective-permute-start(f32[256,8,128]{2,0,1:T(8,128)} %fusion.54), channel_id=1, source_target_pairs={{28,0},{0,4},{4,8},{8,12},{12,16},{16,20},{20,24},{24,28},{29,1},{... | collective-permute-start | bytes 3145736 | tf_op jit(solution)/shard_map/while/body/eval_jaxpr/ppermute | solution.py:13
  457.0 35.0 %collective-permute-start = (bf16[256,8,128]{2,0,1:T(8,128)(2,1)S(1)}, bf16[256,8,128]{2,0,1:T(8,128)(2,1)}, u32[]{:S(2)}, u32[]{:S(2)}) collective-permute-start(bf16[256,8,128]{2,0,1:T(8,128)(2,1)S(1)} %copy.73), channel_id=1, source_target_pairs={{28,0},{0,4},{4,8},{8,12},{12,16},{16,20},{20,24},{24,28},{29,1},{... | collective-permute-start | bytes 1572872 | tf_op jit(solution)/shard_map/while/body/eval_jaxpr/ppermute | solution.py:13
  498.2 37.9 %collective-permute-start.3 = (f32[256,8,128]{2,0,1:T(8,128)}, f32[256,8,128]{2,0,1:T(8,128)}, u32[]{:S(2)}, u32[]{:S(2)}) collective-permute-start(f32[256,8,128]{2,0,1:T(8,128)} %fusion.53), channel_id=1, source_target_pairs={{28,0},{0,4},{4,8},{8,12},{12,16},{16,20},{20,24},{24,28},{29,1},{... | collective-permute-start | bytes 3145736 | tf_op jit(solution)/shard_map/while/body/eval_jaxpr/ppermute | solution.py:13
  501.0 35.2 %collective-permute-start.4 = (f32[256,8,128]{2,0,1:T(8,128)}, f32[256,8,128]{2,0,1:T(8,128)}, u32[]{:S(2)}, u32[]{:S(2)}) collective-permute-start(f32[256,8,128]{2,0,1:T(8,128)} %fusion.54), channel_id=1, source_target_pairs={{28,0},{0,4},{4,8},{8,12},{12,16},{16,20},{20,24},{24,28},{29,1},{... | collective-permute-start | bytes 3145736 | tf_op jit(solution)/shard_map/while/body/eval_jaxpr/ppermute | solution.py:13
  501.0 35.2 %collective-permute-start = (bf16[256,8,128]{2,0,1:T(8,128)(2,1)S(1)}, bf16[256,8,128]{2,0,1:T(8,128)(2,1)}, u32[]{:S(2)}, u32[]{:S(2)}) collective-permute-start(bf16[256,8,128]{2,0,1:T(8,128)(2,1)S(1)} %copy.73), channel_id=1, source_target_pairs={{28,0},{0,4},{4,8},{8,12},{12,16},{16,20},{20,24},{24,28},{29,1},{... | collective-permute-start | bytes 1572872 | tf_op jit(solution)/shard_map/while/body/eval_jaxpr/ppermute | solution.py:13
  542.3 37.9 %collective-permute-start.3 = (f32[256,8,128]{2,0,1:T(8,128)}, f32[256,8,128]{2,0,1:T(8,128)}, u32[]{:S(2)}, u32[]{:S(2)}) collective-permute-start(f32[256,8,128]{2,0,1:T(8,128)} %fusion.53), channel_id=1, source_target_pairs={{28,0},{0,4},{4,8},{8,12},{12,16},{16,20},{20,24},{24,28},{29,1},{... | collective-permute-start | bytes 3145736 | tf_op jit(solution)/shard_map/while/body/eval_jaxpr/ppermute | solution.py:13
  545.1 35.2 %collective-permute-start.4 = (f32[256,8,128]{2,0,1:T(8,128)}, f32[256,8,128]{2,0,1:T(8,128)}, u32[]{:S(2)}, u32[]{:S(2)}) collective-permute-start(f32[256,8,128]{2,0,1:T(8,128)} %fusion.54), channel_id=1, source_target_pairs={{28,0},{0,4},{4,8},{8,12},{12,16},{16,20},{20,24},{24,28},{29,1},{... | collective-permute-start | bytes 3145736 | tf_op jit(solution)/shard_map/while/body/eval_jaxpr/ppermute | solution.py:13
  545.1 35.2 %collective-permute-start = (bf16[256,8,128]{2,0,1:T(8,128)(2,1)S(1)}, bf16[256,8,128]{2,0,1:T(8,128)(2,1)}, u32[]{:S(2)}, u32[]{:S(2)}) collective-permute-start(bf16[256,8,128]{2,0,1:T(8,128)(2,1)S(1)} %copy.73), channel_id=1, source_target_pairs={{28,0},{0,4},{4,8},{8,12},{12,16},{16,20},{20,24},{24,28},{29,1},{... | collective-permute-start | bytes 1572872 | tf_op jit(solution)/shard_map/while/body/eval_jaxpr/ppermute | solution.py:13
  586.4 37.9 %collective-permute-start.3 = (f32[256,8,128]{2,0,1:T(8,128)}, f32[256,8,128]{2,0,1:T(8,128)}, u32[]{:S(2)}, u32[]{:S(2)}) collective-permute-start(f32[256,8,128]{2,0,1:T(8,128)} %fusion.53), channel_id=1, source_target_pairs={{28,0},{0,4},{4,8},{8,12},{12,16},{16,20},{20,24},{24,28},{29,1},{... | collective-permute-start | bytes 3145736 | tf_op jit(solution)/shard_map/while/body/eval_jaxpr/ppermute | solution.py:13
  589.2 35.2 %collective-permute-start.4 = (f32[256,8,128]{2,0,1:T(8,128)}, f32[256,8,128]{2,0,1:T(8,128)}, u32[]{:S(2)}, u32[]{:S(2)}) collective-permute-start(f32[256,8,128]{2,0,1:T(8,128)} %fusion.54), channel_id=1, source_target_pairs={{28,0},{0,4},{4,8},{8,12},{12,16},{16,20},{20,24},{24,28},{29,1},{... | collective-permute-start | bytes 3145736 | tf_op jit(solution)/shard_map/while/body/eval_jaxpr/ppermute | solution.py:13
  589.2 35.2 %collective-permute-start = (bf16[256,8,128]{2,0,1:T(8,128)(2,1)S(1)}, bf16[256,8,128]{2,0,1:T(8,128)(2,1)}, u32[]{:S(2)}, u32[]{:S(2)}) collective-permute-start(bf16[256,8,128]{2,0,1:T(8,128)(2,1)S(1)} %copy.73), channel_id=1, source_target_pairs={{28,0},{0,4},{4,8},{8,12},{12,16},{16,20},{20,24},{24,28},{29,1},{... | collective-permute-start | bytes 1572872 | tf_op jit(solution)/shard_map/while/body/eval_jaxpr/ppermute | solution.py:13
  630.5 37.9 %collective-permute-start.3 = (f32[256,8,128]{2,0,1:T(8,128)}, f32[256,8,128]{2,0,1:T(8,128)}, u32[]{:S(2)}, u32[]{:S(2)}) collective-permute-start(f32[256,8,128]{2,0,1:T(8,128)} %fusion.53), channel_id=1, source_target_pairs={{28,0},{0,4},{4,8},{8,12},{12,16},{16,20},{20,24},{24,28},{29,1},{... | collective-permute-start | bytes 3145736 | tf_op jit(solution)/shard_map/while/body/eval_jaxpr/ppermute | solution.py:13
  633.3 35.2 %collective-permute-start.4 = (f32[256,8,128]{2,0,1:T(8,128)}, f32[256,8,128]{2,0,1:T(8,128)}, u32[]{:S(2)}, u32[]{:S(2)}) collective-permute-start(f32[256,8,128]{2,0,1:T(8,128)} %fusion.54), channel_id=1, source_target_pairs={{28,0},{0,4},{4,8},{8,12},{12,16},{16,20},{20,24},{24,28},{29,1},{... | collective-permute-start | bytes 3145736 | tf_op jit(solution)/shard_map/while/body/eval_jaxpr/ppermute | solution.py:13
  633.3 35.2 %collective-permute-start = (bf16[256,8,128]{2,0,1:T(8,128)(2,1)S(1)}, bf16[256,8,128]{2,0,1:T(8,128)(2,1)}, u32[]{:S(2)}, u32[]{:S(2)}) collective-permute-start(bf16[256,8,128]{2,0,1:T(8,128)(2,1)S(1)} %copy.73), channel_id=1, source_target_pairs={{28,0},{0,4},{4,8},{8,12},{12,16},{16,20},{20,24},{24,28},{29,1},{... | collective-permute-start | bytes 1572872 | tf_op jit(solution)/shard_map/while/body/eval_jaxpr/ppermute | solution.py:13
  (25 other events, 519.3 us)
Sparse Core Ops, SparseCore 0:
  9.9 39.2 all-gather.7
  51.7 37.3 all-gather.5
  90.6 54.7 all-gather.11
  147.2 61.7 all-gather.9
  234.7 52.2 reduce-scatter.2
  291.1 169.2 reduce-scatter.4
where the time goes:
time: 686 us; the launch traced here: 684 us
  waiting for transfers between devices  462 us (67%)
  matrix products  111 us (16%)
  local copies, waits for them, and re-layouts  41.9 us (6%)
  starting transfers between devices  33.5 us (5%)
  between operations  14.3 us (2%)
  blocking collectives  10.4 us (2%)
  other arithmetic  9.66 us (1%)
    ppermute x40, waiting for transfers between devices, shifted(): return lax.ppermute(block, axis, route)  292 us
    all_gather x1, waiting for transfers between devices, shards(): weight_full = lax.all_gather(out_weight, 'seq', axis=1, tiled=True)  63.5 us
    all_gather x1, waiting for transfers between devices, shards(): cotangent_full = lax.all_gather(cotangent, 'fsdp', axis=1, tiled=True)  44.9 us
    all_gather x1, waiting for transfers between devices, shards(): piece_keys = lax.all_gather(key_states, 'seq', axis=0, tiled=True)  33.3 us
    ppermute x40, starting transfers between devices, shifted(): return lax.ppermute(block, axis, route)  33.1 us
    all_gather x1, waiting for transfers between devices, shards(): piece_values = lax.all_gather(value_states, 'seq', axis=0, tiled=True)  26.8 us
    dot_general x8, matrix products, tile_grads(): jnp.einsum('hqk,qhd->khd', probs.astype(jnp.bfloat16), grad_rows, preferr...  22 us
    dot_general x8, matrix products, tile_grads(): jnp.einsum('hqk,qhd->khd', grad_scores, query_rows, preferred_element_typ...  21.7 us
  transfers between devices with their start and end apart: 46, of which 12 were waited for; matrix products, arithmetic and copies ran while one was open for 20% of the time, Pallas kernels for 0%

commit v1 on v0

--- a/solution.py
+++ b/solution.py
@@ -77,7 +77,24 @@
     attn_output = lax.psum_scatter(partial_sum, "fsdp", scatter_dimension=1, tiled=True).astype(
         jnp.float32
     )
-    cotangent_full = lax.all_gather(cotangent, "fsdp", axis=1, tiled=True)
+    ways, here, step = (lax.axis_size("fsdp"), lax.axis_index("fsdp"), cotangent.shape[1])
+    shape = [n * ways if d == 1 else n for d, n in enumerate(cotangent.shape)]
+    cotangent_full = lax.dynamic_update_slice_in_dim(
+        jnp.zeros(shape, cotangent.dtype), cotangent, here * step, axis=1
+    )
+    going_up = going_down = cotangent
+    for far in range(1, ways // 2 + 1):
+        going_up = lax.ppermute(going_up, "fsdp", [(d, (d + 1) % ways) for d in range(ways)])
+        cotangent_full = lax.dynamic_update_slice_in_dim(
+            cotangent_full, going_up, (here - far) % ways * step, axis=1
+        )
+        if 2 * far < ways:
+            going_down = lax.ppermute(
+                going_down, "fsdp", [(d, (d - 1) % ways) for d in range(ways)]
+            )
+            cotangent_full = lax.dynamic_update_slice_in_dim(
+                cotangent_full, going_down, (here + far) % ways * step, axis=1
+            )
     grad_attended = jnp.einsum(
         "td,hd->th", cotangent_full, weight_full, preferred_element_type=jnp.float32
     ).astype(jnp.bfloat16)

time: 686 us -> 630 us (0.918)
  waiting for transfers between devices: 462 us -> 395 us
    all_gather x1 -> x0, waiting for transfers between devices: 44.9 us -> none  [shards(): cotangent_full = lax.all_gather(cotangent, 'fsdp', axis=1, tiled=True)]
    ppermute x0 -> x3, waiting for transfers between devices: none -> 27.7 us  [the longest x2 17.7 us: shards(): lax.ppermute(going_up, 'fsdp', [(d, (d + 1) % ways) for d in range(ways)])]
    all_gather x1, waiting for transfers between devices: 26.8 us -> 0.02 us  [shards(): piece_values = lax.all_gather(value_states, 'seq', axis=0, tiled=True)]
    all_gather x1, waiting for transfers between devices: 63.5 us -> 52.6 us  [shards(): weight_full = lax.all_gather(out_weight, 'seq', axis=1, tiled=True)]
    all_gather x1, waiting for transfers between devices: 33.3 us -> 23 us  [shards(): piece_keys = lax.all_gather(key_states, 'seq', axis=0, tiled=True)]
  transfers between devices with their start and end apart: 46 -> 48, of which waited for: 12 -> 13; matrix products, arithmetic and copies ran while one was open for 20% -> 22% of each run, Pallas kernels for 0% -> 0%
where the time goes in v1:
time: 630 us; the launch traced here: 628 us
  waiting for transfers between devices  395 us (63%)
  matrix products  111 us (18%)
  local copies, waits for them, and re-layouts  48.1 us (8%)
  starting transfers between devices  40.1 us (6%)
  between operations  14.1 us (2%)
  other arithmetic  10.3 us (2%)
  blocking collectives  9.26 us (1%)
    ppermute x40, waiting for transfers between devices, shifted(): return lax.ppermute(block, axis, route)  290 us
    all_gather x1, waiting for transfers between devices, shards(): weight_full = lax.all_gather(out_weight, 'seq', axis=1, tiled=True)  52.6 us
    ppermute x40, starting transfers between devices, shifted(): return lax.ppermute(block, axis, route)  34.5 us
    all_gather x1, waiting for transfers between devices, shards(): piece_keys = lax.all_gather(key_states, 'seq', axis=0, tiled=True)  23 us
    dot_general x8, matrix products, tile_grads(): jnp.einsum('hqk,qhd->khd', grad_scores, query_rows, preferred_element_typ...  21.9 us
    dot_general x8, matrix products, tile_grads(): jnp.einsum('hqk,qhd->khd', probs.astype(jnp.bfloat16), grad_rows, preferr...  21.9 us
    dot_general x8, matrix products, tile_grads(): jnp.einsum('hqk,khd->qhd', grad_scores, key_rows, preferred_element_type=...  19.9 us
    ppermute x2, waiting for transfers between devices, shards(): lax.ppermute(going_up, 'fsdp', [(d, (d + 1) % ways) for d in range(ways)])  17.7 us
  transfers between devices with their start and end apart: 48, of which 13 were waited for; matrix products, arithmetic and copies ran while one was open for 22% of the time, Pallas kernels for 0%

profile of v1, /device:TPU:0, one launch (start us, length us, event | category | flops | bytes accessed | tf_op | source)
XLA Modules:
  0.0 628.0 jit_solution(5550214032742958116)
XLA Ops:
  10.8 3.1 collective-permute-start.5
  16.0 9.3 %all-gather = s32[8,1,256]{2,1,0:T(1,128)S(1)} all-gather(s32[1,1,256]{2,1,0:T(1,128)} %bitcast.97), channel_id=1, replica_groups=mesh['seq'=8,'fsdp'=4] {'seq'}, dimensions={0}, use_global_device_ids=true | all-gather | bytes 9216 | tf_op jit(solution)/shard_map/all_gather | solution.py:65
  27.4 4.5 collective-permute-done.5
  34.7 10.0 %collective-permute-done.6 = bf16[256,1280]{1,0:T(8,128)(2,1)} collective-permute-done((bf16[256,1280]{1,0:T(8,128)(2,1)}, bf16[256,1280]{1,0:T(8,128)(2,1)}, u32[]{:S(2)}, u32[]{:S(2)}) %collective-permute-start.6) | collective-permute-done | bytes 655392 | tf_op jit(solution)/shard_map/ppermute | solution.py:92
  45.9 13.1 %collective-permute-done.7 = bf16[256,1280]{1,0:T(8,128)(2,1)S(1)} collective-permute-done((bf16[256,1280]{1,0:T(8,128)(2,1)}, bf16[256,1280]{1,0:T(8,128)(2,1)S(1)}, u32[]{:S(2)}, u32[]{:S(2)}) %collective-permute-start.7) | collective-permute-done | bytes 655392 | tf_op jit(solution)/shard_map/ppermute | solution.py:87
  59.1 6.9 %copy.42 = bf16[2048,1024]{0,1:T(8,128)(2,1)} copy(bf16[2048,1024]{1,0:T(8,128)(2,1)} %all-gather.7.cloned.1.call-done) | data formatting | bytes 8388608 | tf_op jit(solution)/shard_map/all_gather | solution.py:64
  66.1 23.0 %all-gather.5.cloned.1.call-done = bf16[2048,1024]{0,1:T(8,128)(2,1)} async-done(((bf16[256,1024]{0,1:T(8,128)(2,1)}), bf16[2048,1024]{0,1:T(8,128)(2,1)}) %all-gather.5.cloned.1.call-update) | async-done | bytes 4194320 | tf_op jit(solution)/shard_map/all_gather | solution.py:63
  89.0 5.4 fusion.4
  94.5 4.5 exponential_reduce_fusion
  101.4 52.6 %all-gather.9.cloned.1.call-done = bf16[1024,5120]{1,0:T(8,128)(2,1)} async-done(((bf16[1024,640]{1,0:T(8,128)(2,1)}), bf16[1024,5120]{1,0:T(8,128)(2,1)}) %all-gather.9.cloned.1.call-update) | async-done | bytes 10485776 | tf_op jit(solution)/shard_map/all_gather | solution.py:73
  154.0 7.7 %convolution_convert_fusion.1 = bf16[256,1024]{1,0:T(8,128)(2,1)} fusion(bf16[256,5120]{1,0:T(8,128)(2,1)S(1)} %constant_dynamic-update-slice_fusion, bf16[1024,5120]{1,0:T(8,128)(2,1)} %all-gather.9.cloned.1.call-done), kind=kOutput, calls=%fused_computation.18 | convolution fusion | flops 2684616704 | bytes 13631488 | tf_op jit(solution)/shard_map/td,hd->th/dot_general | solution.py:98
  163.8 9.9 %multiply_reduce_fusion = (f32[256,8]{0,1:T(8,128)S(1)}, bf16[8,256,128]{1,2,0:T(8,128)(2,1)S(1)}) fusion(bf16[256,1024]{0,1:T(8,128)(2,1)} %copy.45, bf16[2048,8,128]{0,2,1:T(8,128)(2,1)} %bitcast.89, f32[8,256,2048]{2,1,0:T(8,128)} %copy-done, f32[8,256]{1,0:T(8,128)S(1)} %log_add_fusion, pred[256,2048]{1,0:T(8,128)(4,1)S(1)} %broadcast_compare_fusion.1), kind=kOutput, calls=%fused_computation.24 | convolution fusion | flops 1091827712 | bytes 22560768 | tf_op jit(solution)/shard_map/hqk,khd->qhd/dot_general | solution.py:68
  174.6 4.3 convolution_convert_fusion
  180.6 9.8 %fusion.10 = f32[1024,5120]{1,0:T(8,128)} fusion(bf16[256,1024]{0,1:T(8,128)(2,1)} %bitcast.91, bf16[256,5120]{1,0:T(8,128)(2,1)S(1)} %copy-done.2), kind=kOutput, calls=%fused_computation.34 | convolution fusion | flops 2684354560 | bytes 24117248 | tf_op jit(solution)/shard_map/th,td->hd/dot_general | solution.py:101
  196.4 416.6 %while.21 = (s32[]{:T(128)}, bf16[256,8,128]{2,0,1:T(8,128)(2,1)}, bf16[256,8,128]{2,0,1:T(8,128)(2,1)}, s32[256]{0:T(256)S(1)}, f32[256,8,128]{2,0,1:T(8,128)},...) while((s32[]{:T(128)}, bf16[256,8,128]{2,0,1:T(8,128)(2,1)}, ...), condition=%wide.region_5.6_spmd.clone, body=%wide.region_4.5_spmd.clone.sunk | while | flops 675872768 | bytes 34234708 | solution.py:127
  209.8 30.6 %collective-permute-done.2 = s32[256]{0:T(256)S(1)} collective-permute-done((s32[256]{0:T(256)S(1)}, s32[256]{0:T(256)S(1)}, u32[]{:S(2)}, u32[]{:S(2)}) %collective-permute-start.2) | collective-permute-done | bytes 1056 | tf_op jit(solution)/shard_map/while/body/eval_jaxpr/ppermute | solution.py:13
  244.0 3.0 fusion.53
  246.9 2.9 fusion.54
  255.9 43.7 %collective-permute-done.2 = s32[256]{0:T(256)S(1)} collective-permute-done((s32[256]{0:T(256)S(1)}, s32[256]{0:T(256)S(1)}, u32[]{:S(2)}, u32[]{:S(2)}) %collective-permute-start.2) | collective-permute-done | bytes 1056 | tf_op jit(solution)/shard_map/while/body/eval_jaxpr/ppermute | solution.py:13
  303.1 2.8 fusion.53
  310.0 3.5 collective-permute-start.1
  316.1 75.9 %collective-permute-done.2 = s32[256]{0:T(256)S(1)} collective-permute-done((s32[256]{0:T(256)S(1)}, s32[256]{0:T(256)S(1)}, u32[]{:S(2)}, u32[]{:S(2)}) %collective-permute-start.2) | collective-permute-done | bytes 1056 | tf_op jit(solution)/shard_map/while/body/eval_jaxpr/ppermute | solution.py:13
  402.5 3.4 collective-permute-start.1
  408.6 28.0 %collective-permute-done.2 = s32[256]{0:T(256)S(1)} collective-permute-done((s32[256]{0:T(256)S(1)}, s32[256]{0:T(256)S(1)}, u32[]{:S(2)}, u32[]{:S(2)}) %collective-permute-start.2) | collective-permute-done | bytes 1056 | tf_op jit(solution)/shard_map/while/body/eval_jaxpr/ppermute | solution.py:13
  446.6 3.4 collective-permute-start.1
  452.7 28.0 %collective-permute-done.2 = s32[256]{0:T(256)S(1)} collective-permute-done((s32[256]{0:T(256)S(1)}, s32[256]{0:T(256)S(1)}, u32[]{:S(2)}, u32[]{:S(2)}) %collective-permute-start.2) | collective-permute-done | bytes 1056 | tf_op jit(solution)/shard_map/while/body/eval_jaxpr/ppermute | solution.py:13
  490.7 3.4 collective-permute-start.1
  496.8 28.0 %collective-permute-done.2 = s32[256]{0:T(256)S(1)} collective-permute-done((s32[256]{0:T(256)S(1)}, s32[256]{0:T(256)S(1)}, u32[]{:S(2)}, u32[]{:S(2)}) %collective-permute-start.2) | collective-permute-done | bytes 1056 | tf_op jit(solution)/shard_map/while/body/eval_jaxpr/ppermute | solution.py:13
  534.8 3.4 collective-permute-start.1
  540.9 28.0 %collective-permute-done.2 = s32[256]{0:T(256)S(1)} collective-permute-done((s32[256]{0:T(256)S(1)}, s32[256]{0:T(256)S(1)}, u32[]{:S(2)}, u32[]{:S(2)}) %collective-permute-start.2) | collective-permute-done | bytes 1056 | tf_op jit(solution)/shard_map/while/body/eval_jaxpr/ppermute | solution.py:13
  578.9 3.4 collective-permute-start.1
  585.0 28.0 %collective-permute-done.2 = s32[256]{0:T(256)S(1)} collective-permute-done((s32[256]{0:T(256)S(1)}, s32[256]{0:T(256)S(1)}, u32[]{:S(2)}, u32[]{:S(2)}) %collective-permute-start.2) | collective-permute-done | bytes 1056 | tf_op jit(solution)/shard_map/while/body/eval_jaxpr/ppermute | solution.py:13
  (202 shorter events, 129.9 us)
Async XLA Ops:
  7.2 52.0 %all-gather.7.cloned.1.call-start = ((), (), s32[]{:S(2)}) async-start(), calls=%async_computation.3 | async-start | bytes 4718592 | tf_op jit(solution)/shard_map/all_gather | solution.py:64
  7.9 81.1 %all-gather.5.cloned.1.call-start = ((), (), s32[]{:S(2)}) async-start(), calls=%async_computation.2 | async-start | bytes 4718592 | tf_op jit(solution)/shard_map/all_gather | solution.py:63
  10.0 143.9 %all-gather.9.cloned.1.call-start = ((), (), s32[]{:S(2)}) async-start(), calls=%async_computation.4 | async-start | bytes 11796480 | tf_op jit(solution)/shard_map/all_gather | solution.py:73
  10.8 608.5 %reduce-scatter.3.cloned.1.call-start = ((), (), s32[]{:S(2)}) async-start(), calls=%async_computation.5 | async-start | bytes 3276800 | tf_op jit(solution)/shard_map/reduce_scatter | solution.py:77
  178.8 442.6 %reduce-scatter.5.cloned.1.call-start = ((), (), s32[]{:S(2)}) async-start(), calls=%async_computation.6 | async-start | bytes 23592960 | tf_op jit(solution)/shard_map/reduce_scatter | solution.py:104
  202.5 37.9 %collective-permute-start.3 = (f32[256,8,128]{2,0,1:T(8,128)}, f32[256,8,128]{2,0,1:T(8,128)}, u32[]{:S(2)}, u32[]{:S(2)}) collective-permute-start(f32[256,8,128]{2,0,1:T(8,128)} %fusion.53), channel_id=1, source_target_pairs={{28,0},{0,4},{4,8},{8,12},{12,16},{16,20},{20,24},{24,28},{29,1},{... | collective-permute-start | bytes 3145736 | tf_op jit(solution)/shard_map/while/body/eval_jaxpr/ppermute | solution.py:13
  205.6 34.9 %collective-permute-start.4 = (f32[256,8,128]{2,0,1:T(8,128)}, f32[256,8,128]{2,0,1:T(8,128)}, u32[]{:S(2)}, u32[]{:S(2)}) collective-permute-start(f32[256,8,128]{2,0,1:T(8,128)} %fusion.54), channel_id=1, source_target_pairs={{28,0},{0,4},{4,8},{8,12},{12,16},{16,20},{20,24},{24,28},{29,1},{... | collective-permute-start | bytes 3145736 | tf_op jit(solution)/shard_map/while/body/eval_jaxpr/ppermute | solution.py:13
  246.9 52.6 %collective-permute-start.3 = (f32[256,8,128]{2,0,1:T(8,128)}, f32[256,8,128]{2,0,1:T(8,128)}, u32[]{:S(2)}, u32[]{:S(2)}) collective-permute-start(f32[256,8,128]{2,0,1:T(8,128)} %fusion.53), channel_id=1, source_target_pairs={{28,0},{0,4},{4,8},{8,12},{12,16},{16,20},{20,24},{24,28},{29,1},{... | collective-permute-start | bytes 3145736 | tf_op jit(solution)/shard_map/while/body/eval_jaxpr/ppermute | solution.py:13
  249.8 49.8 %collective-permute-start.4 = (f32[256,8,128]{2,0,1:T(8,128)}, f32[256,8,128]{2,0,1:T(8,128)}, u32[]{:S(2)}, u32[]{:S(2)}) collective-permute-start(f32[256,8,128]{2,0,1:T(8,128)} %fusion.54), channel_id=1, source_target_pairs={{28,0},{0,4},{4,8},{8,12},{12,16},{16,20},{20,24},{24,28},{29,1},{... | collective-permute-start | bytes 3145736 | tf_op jit(solution)/shard_map/while/body/eval_jaxpr/ppermute | solution.py:13
  250.8 48.7 %collective-permute-start = (bf16[256,8,128]{2,0,1:T(8,128)(2,1)S(1)}, bf16[256,8,128]{2,0,1:T(8,128)(2,1)}, u32[]{:S(2)}, u32[]{:S(2)}) collective-permute-start(bf16[256,8,128]{2,0,1:T(8,128)(2,1)S(1)} %copy.77), channel_id=1, source_target_pairs={{28,0},{0,4},{4,8},{8,12},{12,16},{16,20},{20,24},{24,28},{29,1},{... | collective-permute-start | bytes 1572872 | tf_op jit(solution)/shard_map/while/body/eval_jaxpr/ppermute | solution.py:13
  250.8 48.7 %collective-permute-start.1 = (bf16[256,8,128]{2,0,1:T(8,128)(2,1)S(1)}, bf16[256,8,128]{2,0,1:T(8,128)(2,1)}, u32[]{:S(2)}, u32[]{:S(2)}) collective-permute-start(bf16[256,8,128]{2,0,1:T(8,128)(2,1)S(1)} %copy.78), channel_id=1, source_target_pairs={{28,0},{0,4},{4,8},{8,12},{12,16},{16,20},{20,24},{24,28},{29,1},{... | collective-permute-start | bytes 1572872 | tf_op jit(solution)/shard_map/while/body/eval_jaxpr/ppermute | solution.py:13
  253.1 46.5 %collective-permute-start.2 = (s32[256]{0:T(256)S(1)}, s32[256]{0:T(256)S(1)}, u32[]{:S(2)}, u32[]{:S(2)}) collective-permute-start(s32[256]{0:T(256)S(1)} %copy.79), channel_id=1, source_target_pairs={{28,0},{0,4},{4,8},{8,12},{12,16},{16,20},{20,24},{24,28},{29,1},{... | collective-permute-start | bytes 3080 | tf_op jit(solution)/shard_map/while/body/eval_jaxpr/ppermute | solution.py:13
  306.0 86.1 %collective-permute-start.3 = (f32[256,8,128]{2,0,1:T(8,128)}, f32[256,8,128]{2,0,1:T(8,128)}, u32[]{:S(2)}, u32[]{:S(2)}) collective-permute-start(f32[256,8,128]{2,0,1:T(8,128)} %fusion.53), channel_id=1, source_target_pairs={{28,0},{0,4},{4,8},{8,12},{12,16},{16,20},{20,24},{24,28},{29,1},{... | collective-permute-start | bytes 3145736 | tf_op jit(solution)/shard_map/while/body/eval_jaxpr/ppermute | solution.py:13
  308.7 83.4 %collective-permute-start.4 = (f32[256,8,128]{2,0,1:T(8,128)}, f32[256,8,128]{2,0,1:T(8,128)}, u32[]{:S(2)}, u32[]{:S(2)}) collective-permute-start(f32[256,8,128]{2,0,1:T(8,128)} %fusion.54), channel_id=1, source_target_pairs={{28,0},{0,4},{4,8},{8,12},{12,16},{16,20},{20,24},{24,28},{29,1},{... | collective-permute-start | bytes 3145736 | tf_op jit(solution)/shard_map/while/body/eval_jaxpr/ppermute | solution.py:13
  309.9 82.2 %collective-permute-start = (bf16[256,8,128]{2,0,1:T(8,128)(2,1)S(1)}, bf16[256,8,128]{2,0,1:T(8,128)(2,1)}, u32[]{:S(2)}, u32[]{:S(2)}) collective-permute-start(bf16[256,8,128]{2,0,1:T(8,128)(2,1)S(1)} %copy.77), channel_id=1, source_target_pairs={{28,0},{0,4},{4,8},{8,12},{12,16},{16,20},{20,24},{24,28},{29,1},{... | collective-permute-start | bytes 1572872 | tf_op jit(solution)/shard_map/while/body/eval_jaxpr/ppermute | solution.py:13
  310.0 82.0 %collective-permute-start.1 = (bf16[256,8,128]{2,0,1:T(8,128)(2,1)S(1)}, bf16[256,8,128]{2,0,1:T(8,128)(2,1)}, u32[]{:S(2)}, u32[]{:S(2)}) collective-permute-start(bf16[256,8,128]{2,0,1:T(8,128)(2,1)S(1)} %copy.78), channel_id=1, source_target_pairs={{28,0},{0,4},{4,8},{8,12},{12,16},{16,20},{20,24},{24,28},{29,1},{... | collective-permute-start | bytes 1572872 | tf_op jit(solution)/shard_map/while/body/eval_jaxpr/ppermute | solution.py:13
  313.5 78.6 %collective-permute-start.2 = (s32[256]{0:T(256)S(1)}, s32[256]{0:T(256)S(1)}, u32[]{:S(2)}, u32[]{:S(2)}) collective-permute-start(s32[256]{0:T(256)S(1)} %copy.79), channel_id=1, source_target_pairs={{28,0},{0,4},{4,8},{8,12},{12,16},{16,20},{20,24},{24,28},{29,1},{... | collective-permute-start | bytes 3080 | tf_op jit(solution)/shard_map/while/body/eval_jaxpr/ppermute | solution.py:13
  398.3 38.3 %collective-permute-start.3 = (f32[256,8,128]{2,0,1:T(8,128)}, f32[256,8,128]{2,0,1:T(8,128)}, u32[]{:S(2)}, u32[]{:S(2)}) collective-permute-start(f32[256,8,128]{2,0,1:T(8,128)} %fusion.53), channel_id=1, source_target_pairs={{28,0},{0,4},{4,8},{8,12},{12,16},{16,20},{20,24},{24,28},{29,1},{... | collective-permute-start | bytes 3145736 | tf_op jit(solution)/shard_map/while/body/eval_jaxpr/ppermute | solution.py:13
  401.0 35.5 %collective-permute-start.4 = (f32[256,8,128]{2,0,1:T(8,128)}, f32[256,8,128]{2,0,1:T(8,128)}, u32[]{:S(2)}, u32[]{:S(2)}) collective-permute-start(f32[256,8,128]{2,0,1:T(8,128)} %fusion.54), channel_id=1, source_target_pairs={{28,0},{0,4},{4,8},{8,12},{12,16},{16,20},{20,24},{24,28},{29,1},{... | collective-permute-start | bytes 3145736 | tf_op jit(solution)/shard_map/while/body/eval_jaxpr/ppermute | solution.py:13
  402.3 34.2 %collective-permute-start = (bf16[256,8,128]{2,0,1:T(8,128)(2,1)S(1)}, bf16[256,8,128]{2,0,1:T(8,128)(2,1)}, u32[]{:S(2)}, u32[]{:S(2)}) collective-permute-start(bf16[256,8,128]{2,0,1:T(8,128)(2,1)S(1)} %copy.77), channel_id=1, source_target_pairs={{28,0},{0,4},{4,8},{8,12},{12,16},{16,20},{20,24},{24,28},{29,1},{... | collective-permute-start | bytes 1572872 | tf_op jit(solution)/shard_map/while/body/eval_jaxpr/ppermute | solution.py:13
  442.8 37.9 %collective-permute-start.3 = (f32[256,8,128]{2,0,1:T(8,128)}, f32[256,8,128]{2,0,1:T(8,128)}, u32[]{:S(2)}, u32[]{:S(2)}) collective-permute-start(f32[256,8,128]{2,0,1:T(8,128)} %fusion.53), channel_id=1, source_target_pairs={{28,0},{0,4},{4,8},{8,12},{12,16},{16,20},{20,24},{24,28},{29,1},{... | collective-permute-start | bytes 3145736 | tf_op jit(solution)/shard_map/while/body/eval_jaxpr/ppermute | solution.py:13
  445.5 35.2 %collective-permute-start.4 = (f32[256,8,128]{2,0,1:T(8,128)}, f32[256,8,128]{2,0,1:T(8,128)}, u32[]{:S(2)}, u32[]{:S(2)}) collective-permute-start(f32[256,8,128]{2,0,1:T(8,128)} %fusion.54), channel_id=1, source_target_pairs={{28,0},{0,4},{4,8},{8,12},{12,16},{16,20},{20,24},{24,28},{29,1},{... | collective-permute-start | bytes 3145736 | tf_op jit(solution)/shard_map/while/body/eval_jaxpr/ppermute | solution.py:13
  445.6 35.1 %collective-permute-start = (bf16[256,8,128]{2,0,1:T(8,128)(2,1)S(1)}, bf16[256,8,128]{2,0,1:T(8,128)(2,1)}, u32[]{:S(2)}, u32[]{:S(2)}) collective-permute-start(bf16[256,8,128]{2,0,1:T(8,128)(2,1)S(1)} %copy.77), channel_id=1, source_target_pairs={{28,0},{0,4},{4,8},{8,12},{12,16},{16,20},{20,24},{24,28},{29,1},{... | collective-permute-start | bytes 1572872 | tf_op jit(solution)/shard_map/while/body/eval_jaxpr/ppermute | solution.py:13
  486.9 37.9 %collective-permute-start.3 = (f32[256,8,128]{2,0,1:T(8,128)}, f32[256,8,128]{2,0,1:T(8,128)}, u32[]{:S(2)}, u32[]{:S(2)}) collective-permute-start(f32[256,8,128]{2,0,1:T(8,128)} %fusion.53), channel_id=1, source_target_pairs={{28,0},{0,4},{4,8},{8,12},{12,16},{16,20},{20,24},{24,28},{29,1},{... | collective-permute-start | bytes 3145736 | tf_op jit(solution)/shard_map/while/body/eval_jaxpr/ppermute | solution.py:13
  489.6 35.2 %collective-permute-start.4 = (f32[256,8,128]{2,0,1:T(8,128)}, f32[256,8,128]{2,0,1:T(8,128)}, u32[]{:S(2)}, u32[]{:S(2)}) collective-permute-start(f32[256,8,128]{2,0,1:T(8,128)} %fusion.54), channel_id=1, source_target_pairs={{28,0},{0,4},{4,8},{8,12},{12,16},{16,20},{20,24},{24,28},{29,1},{... | collective-permute-start | bytes 3145736 | tf_op jit(solution)/shard_map/while/body/eval_jaxpr/ppermute | solution.py:13
  489.6 35.2 %collective-permute-start = (bf16[256,8,128]{2,0,1:T(8,128)(2,1)S(1)}, bf16[256,8,128]{2,0,1:T(8,128)(2,1)}, u32[]{:S(2)}, u32[]{:S(2)}) collective-permute-start(bf16[256,8,128]{2,0,1:T(8,128)(2,1)S(1)} %copy.77), channel_id=1, source_target_pairs={{28,0},{0,4},{4,8},{8,12},{12,16},{16,20},{20,24},{24,28},{29,1},{... | collective-permute-start | bytes 1572872 | tf_op jit(solution)/shard_map/while/body/eval_jaxpr/ppermute | solution.py:13
  531.0 37.9 %collective-permute-start.3 = (f32[256,8,128]{2,0,1:T(8,128)}, f32[256,8,128]{2,0,1:T(8,128)}, u32[]{:S(2)}, u32[]{:S(2)}) collective-permute-start(f32[256,8,128]{2,0,1:T(8,128)} %fusion.53), channel_id=1, source_target_pairs={{28,0},{0,4},{4,8},{8,12},{12,16},{16,20},{20,24},{24,28},{29,1},{... | collective-permute-start | bytes 3145736 | tf_op jit(solution)/shard_map/while/body/eval_jaxpr/ppermute | solution.py:13
  533.7 35.2 %collective-permute-start.4 = (f32[256,8,128]{2,0,1:T(8,128)}, f32[256,8,128]{2,0,1:T(8,128)}, u32[]{:S(2)}, u32[]{:S(2)}) collective-permute-start(f32[256,8,128]{2,0,1:T(8,128)} %fusion.54), channel_id=1, source_target_pairs={{28,0},{0,4},{4,8},{8,12},{12,16},{16,20},{20,24},{24,28},{29,1},{... | collective-permute-start | bytes 3145736 | tf_op jit(solution)/shard_map/while/body/eval_jaxpr/ppermute | solution.py:13
  533.7 35.2 %collective-permute-start = (bf16[256,8,128]{2,0,1:T(8,128)(2,1)S(1)}, bf16[256,8,128]{2,0,1:T(8,128)(2,1)}, u32[]{:S(2)}, u32[]{:S(2)}) collective-permute-start(bf16[256,8,128]{2,0,1:T(8,128)(2,1)S(1)} %copy.77), channel_id=1, source_target_pairs={{28,0},{0,4},{4,8},{8,12},{12,16},{16,20},{20,24},{24,28},{29,1},{... | collective-permute-start | bytes 1572872 | tf_op jit(solution)/shard_map/while/body/eval_jaxpr/ppermute | solution.py:13
  575.1 37.9 %collective-permute-start.3 = (f32[256,8,128]{2,0,1:T(8,128)}, f32[256,8,128]{2,0,1:T(8,128)}, u32[]{:S(2)}, u32[]{:S(2)}) collective-permute-start(f32[256,8,128]{2,0,1:T(8,128)} %fusion.53), channel_id=1, source_target_pairs={{28,0},{0,4},{4,8},{8,12},{12,16},{16,20},{20,24},{24,28},{29,1},{... | collective-permute-start | bytes 3145736 | tf_op jit(solution)/shard_map/while/body/eval_jaxpr/ppermute | solution.py:13
  577.8 35.2 %collective-permute-start.4 = (f32[256,8,128]{2,0,1:T(8,128)}, f32[256,8,128]{2,0,1:T(8,128)}, u32[]{:S(2)}, u32[]{:S(2)}) collective-permute-start(f32[256,8,128]{2,0,1:T(8,128)} %fusion.54), channel_id=1, source_target_pairs={{28,0},{0,4},{4,8},{8,12},{12,16},{16,20},{20,24},{24,28},{29,1},{... | collective-permute-start | bytes 3145736 | tf_op jit(solution)/shard_map/while/body/eval_jaxpr/ppermute | solution.py:13
  577.8 35.2 %collective-permute-start = (bf16[256,8,128]{2,0,1:T(8,128)(2,1)S(1)}, bf16[256,8,128]{2,0,1:T(8,128)(2,1)}, u32[]{:S(2)}, u32[]{:S(2)}) collective-permute-start(bf16[256,8,128]{2,0,1:T(8,128)(2,1)S(1)} %copy.77), channel_id=1, source_target_pairs={{28,0},{0,4},{4,8},{8,12},{12,16},{16,20},{20,24},{24,28},{29,1},{... | collective-permute-start | bytes 1572872 | tf_op jit(solution)/shard_map/while/body/eval_jaxpr/ppermute | solution.py:13
  (29 other events, 667.4 us)
Sparse Core Ops, SparseCore 0:
  9.9 39.2 all-gather.6
  51.7 37.3 all-gather.4
  90.9 62.9 all-gather.8
  179.0 52.2 reduce-scatter.2
  235.3 169.2 reduce-scatter.4
